TPU v7x, 128 devices: a whole 4x4x4 slice. The times are simulated.
128 devices in a mesh: seq: 32 (over x, y, core), fsdp: 4 (over z).
Axes of the slice: x: 4, y: 4, z: 4, core: 2. Of those that a mesh axis runs over, the one named last changes fastest.
Arguments:
- patches: bfloat16 [32768, 1280], P(('seq', 'fsdp')), may hold values from -6 to 6
- vis_index: int32 [32768], P(('seq', 'fsdp')), may hold values from 0 to 131071, as said below
- kv_list: int32 [256, 16], P(('seq', 'fsdp')), may hold values from 0 to 255, as said below
- kv_count: int32 [256], P(('seq', 'fsdp')), may hold values from 1 to 16, as said below
- global_tiles: int32 [2], replicated, may hold values from 0 to 255
- frame_table: bfloat16 [256, 1280], replicated, may hold values from -3 to 3
- space_table: bfloat16 [512, 1280], replicated, may hold values from -3 to 3
- ln_gain: bfloat16 [1280], replicated, may hold values from 0.25 to 1.75
- ln_bias: bfloat16 [1280], replicated, may hold values from -3 to 3
- w_qkv: bfloat16 [1280, 3840], P('fsdp')
- w_out: bfloat16 [1280, 1280], P('fsdp'), may hold values from -1.25 to 1.25
Outputs:
- attended: bfloat16 [32768, 1280], P(('seq', 'fsdp'))
Inputs may be any that keep to these rules, and one draw needn't show every extreme that they name: `vis_index`: exactly one visible position in each aligned group of four; strictly increasing. `kv_list`: the first entry of query tile i is i itself; entries may repeat; every entry t satisfies |t // 8 - i // 8| <= 2. Over all entries of an aligned run of 2 query tiles, the tiles that lie in any one group other than the run's own group (group = tile // 8) number at most 3 distinct ones, and exactly 3 for every such group within two of the run's own. On every device at least one query tile has kv_count = 16.
All inputs are finite; a program needn't handle non-finite values.
Results may differ from a plain program's by a relative error of at most 0.0065.
Values may be sent and summed in bfloat16 or wider, within the bound.
No kernel may reach another device: no remote copies, remote signals or barrier semaphores. Data moves between devices by JAX's collectives and lax.ppermute only.
A program may use at most 192 MiB of HBM per device.

v0:
```python
import jax
import jax.numpy as jnp
from jax import lax
from jax.sharding import PartitionSpec as P

HEADS = 16
TILE = 128
KT = 16
GLOBAL = 2
PATCHES = 512


def passed_along(block, axis, distance):
    devices = range(lax.axis_size(axis))
    route = [(i - distance, i) for i in devices if i - distance in devices]
    return lax.ppermute(block, axis, route)


def broadcast(shard, axis, root):
    mine = lax.axis_index(axis) == root
    return lax.psum(jnp.where(mine, shard, jnp.zeros_like(shard)), axis)


def layer_norm(stream, ln_gain, ln_bias):
    stream32 = stream.astype(jnp.float32)
    mean_val = jnp.mean(stream32, axis=-1, keepdims=True)
    centred = stream32 - mean_val
    variance = jnp.mean(centred * centred, axis=-1, keepdims=True)
    scaled = centred * lax.rsqrt(variance + 1e-06)
    return (scaled * ln_gain.astype(jnp.float32) + ln_bias.astype(jnp.float32)).astype(jnp.bfloat16)


def project(inputs, weight):
    return jnp.dot(
        inputs,
        lax.all_gather(weight, "fsdp", axis=0, tiled=True),
        preferred_element_type=jnp.float32,
    )


def attend_tile(query_tile, key_values, key_live, feat_width):
    head_size = feat_width // HEADS
    key_rows = key_values.shape[0]
    queries_h = query_tile.reshape(TILE, HEADS, head_size)
    keys_h = key_values[:, :feat_width].reshape(key_rows, HEADS, head_size)
    values_h = key_values[:, feat_width:].reshape(key_rows, HEADS, head_size)
    scores = jnp.einsum(
        "qhd,khd->hqk", queries_h, keys_h, preferred_element_type=jnp.float32
    ) * head_size ** (-0.5)
    scores = jnp.where(key_live[None, None, :], scores, -jnp.inf)
    row_max = jnp.max(scores, axis=-1, keepdims=True)
    weights_raw = jnp.exp(scores - row_max)
    probs = (weights_raw / jnp.sum(weights_raw, axis=-1, keepdims=True)).astype(jnp.bfloat16)
    mixed_h = jnp.einsum("hqk,khd->qhd", probs, values_h, preferred_element_type=jnp.float32)
    return mixed_h.reshape(TILE, feat_width).astype(jnp.bfloat16)


def local(
    patches,
    vis_index,
    kv_list,
    kv_count,
    global_tiles,
    frame_table,
    space_table,
    ln_gain,
    ln_bias,
    w_qkv,
    w_out,
):
    tok_rows = patches.shape[0]
    feat_width = patches.shape[1]
    tile_count = tok_rows // TILE
    frame_ids = vis_index // PATCHES
    patch_ids = vis_index % PATCHES
    stream = (
        patches.astype(jnp.float32)
        + frame_table[frame_ids].astype(jnp.float32)
        + space_table[patch_ids].astype(jnp.float32)
    ).astype(jnp.bfloat16)
    normed = layer_norm(stream, ln_gain, ln_bias)
    qkv = project(normed, w_qkv).astype(jnp.bfloat16)
    query = qkv[:, :feat_width]
    keyval = qkv[:, feat_width:]
    group_block = lax.all_gather(keyval, "fsdp", axis=0, tiled=True)
    group_tiles = group_block.shape[0] // TILE
    blocks = []
    for offset in (2, 1, 0, -1, -2):
        if offset == 0:
            blocks.append(group_block)
        else:
            blocks.append(passed_along(group_block, "seq", offset))
    window = jnp.concatenate(blocks, axis=0)
    tile_source = window.reshape(5 * group_tiles, TILE, 2 * feat_width)
    local_lists = kv_list - (lax.axis_index("seq") - 2) * group_tiles
    global_list = []
    for slot_no in range(GLOBAL):
        tile_id = global_tiles[slot_no]
        owner_index = tile_id // tile_count
        tile_piece = lax.dynamic_slice_in_dim(keyval, tile_id % tile_count * TILE, TILE, 0)
        global_list.append(broadcast(tile_piece, ("seq", "fsdp"), owner_index))
    global_kv = jnp.stack(global_list, axis=0)
    query_tiles = query.reshape(tile_count, TILE, feat_width)

    def per_tile(tile_args):
        query_tile, local_ids, live_count = tile_args
        slot_live_row = jnp.concatenate(
            [jnp.arange(KT) < live_count, jnp.ones((GLOBAL,), dtype=bool)]
        )
        key_live = jnp.repeat(slot_live_row, TILE)
        key_values = jnp.concatenate([tile_source[local_ids], global_kv], axis=0).reshape(
            (KT + GLOBAL) * TILE, 2 * feat_width
        )
        return attend_tile(query_tile, key_values, key_live, feat_width)

    heads_out = lax.map(per_tile, (query_tiles, local_lists, kv_count)).reshape(
        tok_rows, feat_width
    )
    return project(heads_out, w_out).astype(jnp.bfloat16)


def solution(mesh):
    return jax.shard_map(
        local,
        mesh=mesh,
        in_specs=(
            P(("seq", "fsdp"), None),
            P(("seq", "fsdp")),
            P(("seq", "fsdp"), None),
            P(("seq", "fsdp")),
            P(),
            P(),
            P(),
            P(),
            P(),
            P("fsdp", None),
            P("fsdp", None),
        ),
        out_specs=P(("seq", "fsdp"), None),
        check_vma=False,
    )
```

profile of v0, /device:TPU:1, one launch (start us, length us, event | category | flops | bytes accessed | tf_op | source)
XLA Modules:
  0.0 664.7 jit_solution(8370119231040135235)
XLA Ops:
  6.5 0.7 all-gather.4.cloned.1.call-update
  7.3 0.7 convert_element_type.54
  8.0 0.7 convert_element_type.55
  8.7 0.7 compare_select_fusion.2
  9.4 1.3 gather_fusion.1
  10.7 1.2 gather_fusion.2
  12.6 94.7 %all-gather.4.cloned.1.call-done = bf16[1280,3840]{1,0:T(8,128)(2,1)} async-done(((bf16[320,3840]{1,0:T(8,128)(2,1)}), bf16[1280,3840]{1,0:T(8,128)(2,1)}) %all-gather.4.cloned.1.call-update) | async-done | bytes 9830416 | tf_op jit(solution)/shard_map/all_gather | solution.py:36
  107.4 6.6 convolution_convert_fusion
  114.0 1.3 slice.30
  115.4 58.2 %all-gather.6.cloned.1.call-done = bf16[1024,2560]{1,0:T(8,128)(2,1)} async-done(((bf16[256,2560]{1,0:T(8,128)(2,1)}), bf16[1024,2560]{1,0:T(8,128)(2,1)}) %all-gather.6.cloned.1.call-update) | async-done | bytes 5242896 | tf_op jit(solution)/shard_map/all_gather | solution.py:85
  173.6 5.3 collective-permute-start
  178.9 1.9 collective-permute-start.1
  180.8 4.8 collective-permute-start.2
  185.6 1.3 collective-permute-start.3
  192.7 2.6 select_bitcast_fusion
  195.9 281.7 %all-reduce.4.cloned.1.call-done = (bf16[1,128,2560]{2,1,0:T(8,128)(2,1)}, bf16[1,128,2560]{2,1,0:T(8,128)(2,1)}) async-done(((bf16[1,128,2560]{2,1,0:T(8,128)(2,1)}, bf16[1,128,2560]{2,1,0:T(8,128)(2,1)}), (bf16[1,128,2560]{2,1,0:T(8,128)(2,1)}, bf16[1,128,2560]{2,1,0:T(8,128)(2,1)})) %all-reduce.4.cloned.1.call-update) | async-done | bytes 1310736 | tf_op jit(solution)/shard_map/psum | solution.py:21
  477.6 2.5 copy.23
  480.2 3.8 copy.24
  483.9 5.4 constant_dynamic-update-slice_fusion.5
  489.3 5.3 constant_dynamic-update-slice_fusion.4
  494.6 2.7 constant_dynamic-update-slice_fusion.3
  497.3 5.1 constant_dynamic-update-slice_fusion.2
  502.4 5.3 constant_dynamic-update-slice_fusion.1
  507.7 146.3 %while.10 = (s32[]{:T(128)}, bf16[2,128,1280]{2,1,0:T(8,128)(2,1)}, s32[2,16]{1,0:T(2,128)S(1)}, bf16[40,128,2560]{2,1,0:T(8,128)(2,1)}, bf16[1,128,2560]{1,0,2:...) while((s32[]{:T(128)}, bf16[2,128,1280]{2,1,0:T(8,128)(2,1)}, ...), condition=%wide.region_7.8_spmd, body=%wide.region_4.7_spmd.sunk | while | flops 1550224640 | bytes 152462336 | solution.py:116
  507.7 14.1 %gather_fusion = bf16[16,128,2560]{2,1,0:T(8,128)(2,1)} fusion(bf16[40,128,2560]{2,1,0:T(8,128)(2,1)} %get-tuple-element.176, s32[1024]{0:T(1024)S(1)} %pad_clamp_fusion.4), kind=kCustom, calls=%fused_computation.clone.1 | custom fusion | bytes 20971584 | tf_op jit(solution)/shard_map/while/body/eval_jaxpr/gather | solution.py:111
  521.9 2.5 copy.38
  524.4 0.9 copy.39
  525.3 7.8 %pad_maximum_fusion.2 = bf16[18,128,2560]{2,1,0:T(8,128)(2,1)S(1)} fusion(bf16[1,128,2560]{2,1,0:T(8,128)(2,1)S(1)} %copy.38, bf16[1,128,2560]{2,1,0:T(8,128)(2,1)S(1)} %copy.39, bf16[16,128,2560]{2,1,0:T(8,128)(2,1)} %gather_fusion), kind=kLoop, calls=%fused_computation.8.clone.1 | loop fusion | flops 11796480 | bytes 23592960 | tf_op jit(solution)/shard_map/while/body/eval_jaxpr/concatenate | solution.py:111
  533.1 4.7 fusion.46
  537.8 8.9 %copy.42 = bf16[2304,1280]{0,1:T(8,128)(2,1)} copy(bf16[2304,1280]{1,0:T(8,128)(2,1)} %get-tuple-element.150) | data formatting | bytes 11796480 | tf_op jit(solution)/shard_map/while
  546.9 0.6 dynamic_slice.35
  547.4 0.6 iota_compare_fusion.2
  548.2 11.2 %fusion.47 = (f32[16,128]{1,0:T(8,128)S(1)}, f32[16,128,2304]{2,1,0:T(8,128)}) fusion(pred[2304]{0:T(1024)(128)(4,1)S(1)} %broadcast_bitcast_fusion.2, bf16[128,16,80]{0,2,1:T(8,128)(2,1)S(1)} %bitcast.63, bf16[2304,16,80]{0,2,1:T(8,128)(2,1)} %bitcast.60), kind=kOutput, calls=%fused_computation.63.clone.1 | convolution fusion | flops 773851392 | bytes 25110784 | tf_op jit(solution)/shard_map/while/body/eval_jaxpr/sub | solution.py:52
  559.4 8.9 %copy.40 = bf16[2304,1280]{0,1:T(8,128)(2,1)} copy(bf16[2304,1280]{1,0:T(8,128)(2,1)} %get-tuple-element.149) | data formatting | bytes 11796480 | tf_op jit(solution)/shard_map/while
  568.2 11.6 %fusion.48 = bf16[16,80,128]{2,1,0:T(8,128)(2,1)S(1)} fusion(bf16[2304,16,80]{0,2,1:T(8,128)(2,1)} %bitcast.61, f32[16,128,2304]{2,1,0:T(8,128)} %get-tuple-element.151, f32[16,128]{1,0:T(8,128)S(1)} %get-tuple-element.152), kind=kOutput, calls=%fused_computation.14.clone.1 | convolution fusion | flops 764575744 | bytes 25108480 | tf_op jit(solution)/shard_map/while/body/eval_jaxpr/hqk,khd->qhd/dot_general | solution.py:54
  580.1 0.8 copy-done.8
  580.9 14.1 %gather_fusion = bf16[16,128,2560]{2,1,0:T(8,128)(2,1)} fusion(bf16[40,128,2560]{2,1,0:T(8,128)(2,1)} %get-tuple-element.176, s32[1024]{0:T(1024)S(1)} %pad_clamp_fusion.4), kind=kCustom, calls=%fused_computation.clone.1 | custom fusion | bytes 20971584 | tf_op jit(solution)/shard_map/while/body/eval_jaxpr/gather | solution.py:111
  595.0 2.5 copy.38
  597.5 0.9 copy.39
  598.4 7.8 %pad_maximum_fusion.2 = bf16[18,128,2560]{2,1,0:T(8,128)(2,1)S(1)} fusion(bf16[1,128,2560]{2,1,0:T(8,128)(2,1)S(1)} %copy.38, bf16[1,128,2560]{2,1,0:T(8,128)(2,1)S(1)} %copy.39, bf16[16,128,2560]{2,1,0:T(8,128)(2,1)} %gather_fusion), kind=kLoop, calls=%fused_computation.8.clone.1 | loop fusion | flops 11796480 | bytes 23592960 | tf_op jit(solution)/shard_map/while/body/eval_jaxpr/concatenate | solution.py:111
  606.2 4.7 fusion.46
  610.9 8.9 %copy.42 = bf16[2304,1280]{0,1:T(8,128)(2,1)} copy(bf16[2304,1280]{1,0:T(8,128)(2,1)} %get-tuple-element.150) | data formatting | bytes 11796480 | tf_op jit(solution)/shard_map/while
  620.6 0.6 iota_compare_fusion.2
  621.3 11.2 %fusion.47 = (f32[16,128]{1,0:T(8,128)S(1)}, f32[16,128,2304]{2,1,0:T(8,128)}) fusion(pred[2304]{0:T(1024)(128)(4,1)S(1)} %broadcast_bitcast_fusion.2, bf16[128,16,80]{0,2,1:T(8,128)(2,1)S(1)} %bitcast.63, bf16[2304,16,80]{0,2,1:T(8,128)(2,1)} %bitcast.60), kind=kOutput, calls=%fused_computation.63.clone.1 | convolution fusion | flops 773851392 | bytes 25110784 | tf_op jit(solution)/shard_map/while/body/eval_jaxpr/sub | solution.py:52
  632.5 8.9 %copy.40 = bf16[2304,1280]{0,1:T(8,128)(2,1)} copy(bf16[2304,1280]{1,0:T(8,128)(2,1)} %get-tuple-element.149) | data formatting | bytes 11796480 | tf_op jit(solution)/shard_map/while
  641.4 11.6 %fusion.48 = bf16[16,80,128]{2,1,0:T(8,128)(2,1)S(1)} fusion(bf16[2304,16,80]{0,2,1:T(8,128)(2,1)} %bitcast.61, f32[16,128,2304]{2,1,0:T(8,128)} %get-tuple-element.151, f32[16,128]{1,0:T(8,128)S(1)} %get-tuple-element.152), kind=kOutput, calls=%fused_computation.14.clone.1 | convolution fusion | flops 764575744 | bytes 25108480 | tf_op jit(solution)/shard_map/while/body/eval_jaxpr/hqk,khd->qhd/dot_general | solution.py:54
  653.2 0.8 copy-done.8
  654.1 4.1 convolution_convert_fusion.1
  (66 shorter events, 3.7 us)
Async XLA Ops:
  6.5 4.1 copy-start
  6.5 2.8 copy-start.2
  6.5 100.8 %all-gather.4.cloned.1.call-start = ((), (), s32[]{:S(2)}) async-start(), calls=%async_computation | async-start | bytes 12288000 | tf_op jit(solution)/shard_map/all_gather | solution.py:36
  7.3 166.3 %all-gather.6.cloned.1.call-start = ((), (), s32[]{:S(2)}) async-start(), calls=%async_computation.1 | async-start | bytes 6553600 | tf_op jit(solution)/shard_map/all_gather | solution.py:85
  9.4 2.5 copy-start.4
  12.6 174.3 %copy-start.5 = (s32[2]{0:T(128)S(1)}, s32[2]{0:T(128)}, u32[]{:S(2)}) copy-start(s32[2]{0:T(128)} %param.17) | copy-start | bytes 28
  114.0 363.6 %copy-start.3 = (bf16[256,3840]{1,0:T(8,128)(2,1)}, bf16[256,3840]{1,0:T(8,128)(2,1)S(1)}, u32[]{:S(2)}) copy-start(bf16[256,3840]{1,0:T(8,128)(2,1)S(1)} %convolution_convert_fusion) | copy-start | bytes 5898244
  114.0 81.8 %copy-start.6 = (s32[2,16]{1,0:T(2,128)S(1)}, s32[2,16]{1,0:T(2,128)}, u32[]{:S(2)}) copy-start(s32[2,16]{1,0:T(2,128)} %param.15) | copy-start | bytes 388
  115.3 362.3 %all-reduce.4.cloned.1.call-start = ((), (), s32[]{:S(2)}) async-start(), calls=%async_computation.3 | async-start | bytes 2621440 | tf_op jit(solution)/shard_map/psum | solution.py:21
  173.6 310.3 %collective-permute-start = (bf16[1024,2560]{1,0:T(8,128)(2,1)}, bf16[1024,2560]{1,0:T(8,128)(2,1)}, u32[]{:S(2)}, u32[]{:S(2)}) collective-permute-start(bf16[1024,2560]{1,0:T(8,128)(2,1)} %all-gather.6.cloned.1.call-done), channel_id=1, source_target_pairs={{0,8},{4,12},{8,16},{12,20},{16,24},{20,28},{24,32},{28,36},{32,40... | collective-permute-start | bytes 15728648 | tf_op jit(solution)/shard_map/ppermute | solution.py:16
  178.9 310.4 %collective-permute-start.1 = (bf16[1024,2560]{1,0:T(8,128)(2,1)}, bf16[1024,2560]{1,0:T(8,128)(2,1)}, u32[]{:S(2)}, u32[]{:S(2)}) collective-permute-start(bf16[1024,2560]{1,0:T(8,128)(2,1)} %all-gather.6.cloned.1.call-done), channel_id=1, source_target_pairs={{0,4},{4,8},{8,12},{12,16},{16,20},{20,24},{24,28},{28,32},{32,36}... | collective-permute-start | bytes 15728648 | tf_op jit(solution)/shard_map/ppermute | solution.py:16
  180.8 316.4 %collective-permute-start.2 = (bf16[1024,2560]{1,0:T(8,128)(2,1)}, bf16[1024,2560]{1,0:T(8,128)(2,1)}, u32[]{:S(2)}, u32[]{:S(2)}) collective-permute-start(bf16[1024,2560]{1,0:T(8,128)(2,1)} %all-gather.6.cloned.1.call-done), channel_id=1, source_target_pairs={{4,0},{8,4},{12,8},{16,12},{20,16},{24,20},{28,24},{32,28},{36,32}... | collective-permute-start | bytes 15728648 | tf_op jit(solution)/shard_map/ppermute | solution.py:16
  185.6 316.8 %collective-permute-start.3 = (bf16[1024,2560]{1,0:T(8,128)(2,1)}, bf16[1024,2560]{1,0:T(8,128)(2,1)}, u32[]{:S(2)}, u32[]{:S(2)}) collective-permute-start(bf16[1024,2560]{1,0:T(8,128)(2,1)} %all-gather.6.cloned.1.call-done), channel_id=1, source_target_pairs={{8,0},{12,4},{16,8},{20,12},{24,16},{28,20},{32,24},{36,28},{40,32... | collective-permute-start | bytes 15728648 | tf_op jit(solution)/shard_map/ppermute | solution.py:16
  195.3 458.8 %all-gather.8.cloned.1.call-start = ((), (), s32[]{:S(2)}) async-start(), calls=%async_computation.2 | async-start | bytes 4096000 | tf_op jit(solution)/shard_map/all_gather | solution.py:36
  483.9 10.7 %slice-start.1 = ((s8[5242880]{0:T(1024)(128)(4,1)}), s8[4194304]{0:T(1024)(128)(4,1)S(1)}, s32[]{:S(2)}) async-start(s8[5242880]{0:T(1024)(128)(4,1)} %bitcast.66), calls=%async_computation.5 | async-start | bytes 8388608
  489.3 5.3 slice-start.2
  502.4 5.3 slice-start
  502.4 5.3 copy-start.9
  568.2 11.8 %copy-start.7 = (bf16[2,128,1280]{2,1,0:T(8,128)(2,1)S(1)}, bf16[2,128,1280]{2,1,0:T(8,128)(2,1)}, u32[]{:S(2)}) copy-start(bf16[2,128,1280]{2,1,0:T(8,128)(2,1)} %get-tuple-element.164) | copy-start | bytes 1966084 | tf_op jit(solution)/shard_map/while
  580.1 0.8 copy-start.8
  641.4 11.8 %copy-start.7 = (bf16[2,128,1280]{2,1,0:T(8,128)(2,1)S(1)}, bf16[2,128,1280]{2,1,0:T(8,128)(2,1)}, u32[]{:S(2)}) copy-start(bf16[2,128,1280]{2,1,0:T(8,128)(2,1)} %get-tuple-element.164) | copy-start | bytes 1966084 | tf_op jit(solution)/shard_map/while
  653.2 0.8 copy-start.8
  654.1 4.1 copy-start.1
Sparse Core Ops, SparseCore 0:
  9.0 98.3 all-gather.3
  115.4 58.1 all-gather.5
  195.4 282.1 all-reduce.3
  479.1 39.0 all-gather.7
where the time goes:
time: 666 us; the launch traced here: 665 us
  waiting for transfers between devices  436 us (65%)
  local copies, waits for them, and re-layouts  118 us (18%)
  matrix products  56.3 us (8%)
  other arithmetic  22.2 us (3%)
  between operations  18.4 us (3%)
  starting transfers between devices  13.6 us (2%)
    psum x1, waiting for transfers between devices, broadcast(): return lax.psum(jnp.where(mine, shard, jnp.zeros_like(shard)), axis)  282 us
    all_gather x2, waiting for transfers between devices, project(): lax.all_gather(weight, 'fsdp', axis=0, tiled=True)  94.7 us
    all_gather x1, waiting for transfers between devices, local(): group_block = lax.all_gather(keyval, 'fsdp', axis=0, tiled=True)  58.2 us
    while x12, local copies, waits for them, and re-layouts  37.1 us
    gather x2, local copies, waits for them, and re-layouts, per_tile(): tile_source[local_ids]  28.2 us
    dot_general x2, matrix products, attend_tile(): jnp.einsum('hqk,khd->qhd', probs, values_h, preferred_element_type=jnp.fl...  23.2 us
    sub x2, matrix products, attend_tile(): weights_raw = jnp.exp(scores - row_max)  22.4 us
    unnamed x24, local copies, waits for them, and re-layouts  18.5 us
  transfers between devices with their start and end apart: 8, of which 3 were waited for; matrix products, arithmetic and copies ran while one was open for 28% of the time, Pallas kernels for 0%

commit v1 on v0

--- a/solution.py
+++ b/solution.py
@@ -82,7 +82,9 @@
     qkv = project(normed, w_qkv).astype(jnp.bfloat16)
     query = qkv[:, :feat_width]
     keyval = qkv[:, feat_width:]
-    group_block = lax.all_gather(keyval, "fsdp", axis=0, tiled=True)
+    group_block = jnp.concatenate(
+        lax.all_to_all(jnp.stack([keyval] * lax.axis_size("fsdp")), "fsdp", 0, 0), axis=0
+    )
     group_tiles = group_block.shape[0] // TILE
     blocks = []
     for offset in (2, 1, 0, -1, -2):

time: 666 us -> 673 us (1.011)
  blocking collectives: 0 us -> 62.9 us
  waiting for transfers between devices: 436 us -> 378 us
    all_to_all x0 -> x1, blocking collectives: none -> 62.9 us  [local(): lax.all_to_all(jnp.stack([keyval] * lax.axis_size('fsdp')), 'fsdp', 0, 0)]
    all_gather x1 -> x0, waiting for transfers between devices: 58.2 us -> none  [local(): group_block = lax.all_gather(keyval, 'fsdp', axis=0, tiled=True)]
    unnamed x24 -> x20, local copies, waits for them, and re-layouts: 18.5 us -> 20.8 us
  transfers between devices with their start and end apart: 8 -> 7, of which waited for: 3 -> 2; matrix products, arithmetic and copies ran while one was open for 28% -> 27% of each run, Pallas kernels for 0% -> 0%
where the time goes in v1:
time: 673 us; the launch traced here: 671 us
  waiting for transfers between devices  378 us (56%)
  local copies, waits for them, and re-layouts  120 us (18%)
  blocking collectives  62.9 us (9%)
  matrix products  56.4 us (8%)
  other arithmetic  20.9 us (3%)
  between operations  18.4 us (3%)
  starting transfers between devices  14.7 us (2%)
    psum x1, waiting for transfers between devices, broadcast(): return lax.psum(jnp.where(mine, shard, jnp.zeros_like(shard)), axis)  282 us
    all_gather x2, waiting for transfers between devices, project(): lax.all_gather(weight, 'fsdp', axis=0, tiled=True)  94.8 us
    all_to_all x1, blocking collectives, local(): lax.all_to_all(jnp.stack([keyval] * lax.axis_size('fsdp')), 'fsdp', 0, 0)  62.9 us
    while x12, local copies, waits for them, and re-layouts  37 us
    gather x2, local copies, waits for them, and re-layouts, per_tile(): tile_source[local_ids]  28.1 us
    dot_general x2, matrix products, attend_tile(): jnp.einsum('hqk,khd->qhd', probs, values_h, preferred_element_type=jnp.fl...  23.2 us
    sub x2, matrix products, attend_tile(): weights_raw = jnp.exp(scores - row_max)  22.4 us
    unnamed x20, local copies, waits for them, and re-layouts  20.8 us
  transfers between devices with their start and end apart: 7, of which 2 were waited for; matrix products, arithmetic and copies ran while one was open for 27% of the time, Pallas kernels for 0%

profile of v1, /device:TPU:1, one launch (start us, length us, event | category | flops | bytes accessed | tf_op | source)
XLA Modules:
  0.0 670.8 jit_solution(18154443351513502548)
XLA Ops:
  6.5 0.7 all-gather.3.cloned.1.call-update
  7.3 0.7 convert_element_type.54
  8.0 0.7 convert_element_type.55
  8.7 0.7 compare_select_fusion.2
  9.4 1.3 gather_fusion.1
  10.7 1.2 gather_fusion.2
  12.6 94.7 %all-gather.3.cloned.1.call-done = bf16[1280,3840]{1,0:T(8,128)(2,1)} async-done(((bf16[320,3840]{1,0:T(8,128)(2,1)}), bf16[1280,3840]{1,0:T(8,128)(2,1)}) %all-gather.3.cloned.1.call-update) | async-done | bytes 9830416 | tf_op jit(solution)/shard_map/all_gather | solution.py:36
  107.4 6.6 convolution_convert_fusion
  114.6 62.9 %all_to_all.5 = bf16[4,256,2560]{2,1,0:T(8,128)(2,1)} all-to-all(bf16[4,256,2560]{2,1,0:T(8,128)(2,1)S(1)} %stack.6), channel_id=1, replica_groups=mesh['seq'=32,'fsdp'=4] {'fsdp'}, dimensions={0} | all-to-all | bytes 10485760 | tf_op jit(solution)/shard_map/all_to_all | solution.py:86
  177.5 5.4 collective-permute-start
  182.8 3.0 collective-permute-start.1
  185.8 4.8 collective-permute-start.2
  190.6 1.3 collective-permute-start.3
  197.7 1.3 select_bitcast_fusion
  199.8 281.8 %all-reduce.4.cloned.1.call-done = (bf16[1,128,2560]{2,1,0:T(8,128)(2,1)}, bf16[1,128,2560]{2,1,0:T(8,128)(2,1)}) async-done(((bf16[1,128,2560]{2,1,0:T(8,128)(2,1)}, bf16[1,128,2560]{2,1,0:T(8,128)(2,1)}), (bf16[1,128,2560]{2,1,0:T(8,128)(2,1)}, bf16[1,128,2560]{2,1,0:T(8,128)(2,1)})) %all-reduce.4.cloned.1.call-update) | async-done | bytes 1310736 | tf_op jit(solution)/shard_map/psum | solution.py:21
  481.6 2.5 copy.23
  484.1 3.8 copy.24
  487.8 5.1 constant_dynamic-update-slice_fusion.5
  493.0 5.3 constant_dynamic-update-slice_fusion.4
  498.3 5.2 constant_dynamic-update-slice_fusion.3
  503.6 5.1 constant_dynamic-update-slice_fusion.2
  508.7 5.3 constant_dynamic-update-slice_fusion.1
  514.0 146.2 %while.10 = (s32[]{:T(128)}, bf16[2,128,1280]{2,1,0:T(8,128)(2,1)}, s32[2,16]{1,0:T(2,128)S(1)}, bf16[40,128,2560]{2,1,0:T(8,128)(2,1)}, bf16[1,128,2560]{1,0,2:...) while((s32[]{:T(128)}, bf16[2,128,1280]{2,1,0:T(8,128)(2,1)}, ...), condition=%wide.region_7.8_spmd, body=%wide.region_4.7_spmd.sunk | while | flops 1550224640 | bytes 152462336 | solution.py:118
  514.0 14.1 %gather_fusion = bf16[16,128,2560]{2,1,0:T(8,128)(2,1)} fusion(bf16[40,128,2560]{2,1,0:T(8,128)(2,1)} %get-tuple-element.176, s32[1024]{0:T(1024)S(1)} %pad_clamp_fusion.4), kind=kCustom, calls=%fused_computation.clone.1 | custom fusion | bytes 20971584 | tf_op jit(solution)/shard_map/while/body/eval_jaxpr/gather | solution.py:113
  528.1 2.5 copy.38
  530.6 0.9 copy.39
  531.5 7.8 %pad_maximum_fusion.2 = bf16[18,128,2560]{2,1,0:T(8,128)(2,1)S(1)} fusion(bf16[1,128,2560]{2,1,0:T(8,128)(2,1)S(1)} %copy.38, bf16[1,128,2560]{2,1,0:T(8,128)(2,1)S(1)} %copy.39, bf16[16,128,2560]{2,1,0:T(8,128)(2,1)} %gather_fusion), kind=kLoop, calls=%fused_computation.8.clone.1 | loop fusion | flops 11796480 | bytes 23592960 | tf_op jit(solution)/shard_map/while/body/eval_jaxpr/concatenate | solution.py:113
  539.3 4.7 fusion.46
  543.9 8.8 %copy.42 = bf16[2304,1280]{0,1:T(8,128)(2,1)} copy(bf16[2304,1280]{1,0:T(8,128)(2,1)} %get-tuple-element.150) | data formatting | bytes 11796480 | tf_op jit(solution)/shard_map/while
  553.0 0.6 dynamic_slice.35
  553.6 0.6 iota_compare_fusion.2
  554.4 11.2 %fusion.47 = (f32[16,128]{1,0:T(8,128)S(1)}, f32[16,128,2304]{2,1,0:T(8,128)}) fusion(pred[2304]{0:T(1024)(128)(4,1)S(1)} %broadcast_bitcast_fusion.2, bf16[128,16,80]{0,2,1:T(8,128)(2,1)S(1)} %bitcast.64, bf16[2304,16,80]{0,2,1:T(8,128)(2,1)} %bitcast.61), kind=kOutput, calls=%fused_computation.63.clone.1 | convolution fusion | flops 773851392 | bytes 25110784 | tf_op jit(solution)/shard_map/while/body/eval_jaxpr/sub | solution.py:52
  565.6 8.8 %copy.40 = bf16[2304,1280]{0,1:T(8,128)(2,1)} copy(bf16[2304,1280]{1,0:T(8,128)(2,1)} %get-tuple-element.149) | data formatting | bytes 11796480 | tf_op jit(solution)/shard_map/while
  574.4 11.6 %fusion.48 = bf16[16,80,128]{2,1,0:T(8,128)(2,1)S(1)} fusion(bf16[2304,16,80]{0,2,1:T(8,128)(2,1)} %bitcast.62, f32[16,128,2304]{2,1,0:T(8,128)} %get-tuple-element.151, f32[16,128]{1,0:T(8,128)S(1)} %get-tuple-element.152), kind=kOutput, calls=%fused_computation.14.clone.1 | convolution fusion | flops 764575744 | bytes 25108480 | tf_op jit(solution)/shard_map/while/body/eval_jaxpr/hqk,khd->qhd/dot_general | solution.py:54
  586.3 0.8 copy-done.8
  587.1 14.1 %gather_fusion = bf16[16,128,2560]{2,1,0:T(8,128)(2,1)} fusion(bf16[40,128,2560]{2,1,0:T(8,128)(2,1)} %get-tuple-element.176, s32[1024]{0:T(1024)S(1)} %pad_clamp_fusion.4), kind=kCustom, calls=%fused_computation.clone.1 | custom fusion | bytes 20971584 | tf_op jit(solution)/shard_map/while/body/eval_jaxpr/gather | solution.py:113
  601.2 2.5 copy.38
  603.7 0.9 copy.39
  604.6 7.8 %pad_maximum_fusion.2 = bf16[18,128,2560]{2,1,0:T(8,128)(2,1)S(1)} fusion(bf16[1,128,2560]{2,1,0:T(8,128)(2,1)S(1)} %copy.38, bf16[1,128,2560]{2,1,0:T(8,128)(2,1)S(1)} %copy.39, bf16[16,128,2560]{2,1,0:T(8,128)(2,1)} %gather_fusion), kind=kLoop, calls=%fused_computation.8.clone.1 | loop fusion | flops 11796480 | bytes 23592960 | tf_op jit(solution)/shard_map/while/body/eval_jaxpr/concatenate | solution.py:113
  612.4 4.7 fusion.46
  617.0 8.8 %copy.42 = bf16[2304,1280]{0,1:T(8,128)(2,1)} copy(bf16[2304,1280]{1,0:T(8,128)(2,1)} %get-tuple-element.150) | data formatting | bytes 11796480 | tf_op jit(solution)/shard_map/while
  626.1 0.6 dynamic_slice.35
  626.7 0.6 iota_compare_fusion.2
  627.5 11.2 %fusion.47 = (f32[16,128]{1,0:T(8,128)S(1)}, f32[16,128,2304]{2,1,0:T(8,128)}) fusion(pred[2304]{0:T(1024)(128)(4,1)S(1)} %broadcast_bitcast_fusion.2, bf16[128,16,80]{0,2,1:T(8,128)(2,1)S(1)} %bitcast.64, bf16[2304,16,80]{0,2,1:T(8,128)(2,1)} %bitcast.61), kind=kOutput, calls=%fused_computation.63.clone.1 | convolution fusion | flops 773851392 | bytes 25110784 | tf_op jit(solution)/shard_map/while/body/eval_jaxpr/sub | solution.py:52
  638.7 8.8 %copy.40 = bf16[2304,1280]{0,1:T(8,128)(2,1)} copy(bf16[2304,1280]{1,0:T(8,128)(2,1)} %get-tuple-element.149) | data formatting | bytes 11796480 | tf_op jit(solution)/shard_map/while
  647.5 11.6 %fusion.48 = bf16[16,80,128]{2,1,0:T(8,128)(2,1)S(1)} fusion(bf16[2304,16,80]{0,2,1:T(8,128)(2,1)} %bitcast.62, f32[16,128,2304]{2,1,0:T(8,128)} %get-tuple-element.151, f32[16,128]{1,0:T(8,128)S(1)} %get-tuple-element.152), kind=kOutput, calls=%fused_computation.14.clone.1 | convolution fusion | flops 764575744 | bytes 25108480 | tf_op jit(solution)/shard_map/while/body/eval_jaxpr/hqk,khd->qhd/dot_general | solution.py:54
  659.4 0.8 copy-done.8
  660.2 4.1 convolution_convert_fusion.1
  (60 shorter events, 3.7 us)
Async XLA Ops:
  6.5 4.1 copy-start
  6.5 2.8 copy-start.2
  6.5 100.8 %all-gather.3.cloned.1.call-start = ((), (), s32[]{:S(2)}) async-start(), calls=%async_computation.1 | async-start | bytes 12288000 | tf_op jit(solution)/shard_map/all_gather | solution.py:36
  7.3 474.3 %all-reduce.4.cloned.1.call-start = ((), (), s32[]{:S(2)}) async-start(), calls=%async_computation.3 | async-start | bytes 2621440 | tf_op jit(solution)/shard_map/psum | solution.py:21
  9.4 2.5 copy-start.4
  114.0 85.7 %copy-start.3 = (bf16[256,3840]{1,0:T(8,128)(2,1)}, bf16[256,3840]{1,0:T(8,128)(2,1)S(1)}, u32[]{:S(2)}) copy-start(bf16[256,3840]{1,0:T(8,128)(2,1)S(1)} %convolution_convert_fusion) | copy-start | bytes 5898244
  114.5 77.4 %copy-start.5 = (s32[2]{0:T(128)S(1)}, s32[2]{0:T(128)}, u32[]{:S(2)}) copy-start(s32[2]{0:T(128)} %param.17) | copy-start | bytes 28
  114.5 85.2 %copy-start.6 = (s32[2,16]{1,0:T(2,128)S(1)}, s32[2,16]{1,0:T(2,128)}, u32[]{:S(2)}) copy-start(s32[2,16]{1,0:T(2,128)} %param.15) | copy-start | bytes 388
  177.5 310.4 %collective-permute-start = (bf16[1024,2560]{1,0:T(8,128)(2,1)}, bf16[1024,2560]{1,0:T(8,128)(2,1)}, u32[]{:S(2)}, u32[]{:S(2)}) collective-permute-start(bf16[1024,2560]{1,0:T(8,128)(2,1)} %bitcast.10), channel_id=1, source_target_pairs={{0,8},{4,12},{8,16},{12,20},{16,24},{20,28},{24,32},{28,36},{32,40... | collective-permute-start | bytes 15728648 | tf_op jit(solution)/shard_map/ppermute | solution.py:16
  182.8 310.2 %collective-permute-start.1 = (bf16[1024,2560]{1,0:T(8,128)(2,1)}, bf16[1024,2560]{1,0:T(8,128)(2,1)}, u32[]{:S(2)}, u32[]{:S(2)}) collective-permute-start(bf16[1024,2560]{1,0:T(8,128)(2,1)} %bitcast.10), channel_id=1, source_target_pairs={{0,4},{4,8},{8,12},{12,16},{16,20},{20,24},{24,28},{28,32},{32,36}... | collective-permute-start | bytes 15728648 | tf_op jit(solution)/shard_map/ppermute | solution.py:16
  185.8 317.7 %collective-permute-start.2 = (bf16[1024,2560]{1,0:T(8,128)(2,1)}, bf16[1024,2560]{1,0:T(8,128)(2,1)}, u32[]{:S(2)}, u32[]{:S(2)}) collective-permute-start(bf16[1024,2560]{1,0:T(8,128)(2,1)} %bitcast.10), channel_id=1, source_target_pairs={{4,0},{8,4},{12,8},{16,12},{20,16},{24,20},{28,24},{32,28},{36,32}... | collective-permute-start | bytes 15728648 | tf_op jit(solution)/shard_map/ppermute | solution.py:16
  190.6 318.0 %collective-permute-start.3 = (bf16[1024,2560]{1,0:T(8,128)(2,1)}, bf16[1024,2560]{1,0:T(8,128)(2,1)}, u32[]{:S(2)}, u32[]{:S(2)}) collective-permute-start(bf16[1024,2560]{1,0:T(8,128)(2,1)} %bitcast.10), channel_id=1, source_target_pairs={{8,0},{12,4},{16,8},{20,12},{24,16},{28,20},{32,24},{36,28},{40,32... | collective-permute-start | bytes 15728648 | tf_op jit(solution)/shard_map/ppermute | solution.py:16
  199.0 461.2 %all-gather.5.cloned.1.call-start = ((), (), s32[]{:S(2)}) async-start(), calls=%async_computation.2 | async-start | bytes 4096000 | tf_op jit(solution)/shard_map/all_gather | solution.py:36
  508.7 5.3 slice-start
  508.7 5.3 copy-start.9
  574.4 11.8 %copy-start.7 = (bf16[2,128,1280]{2,1,0:T(8,128)(2,1)S(1)}, bf16[2,128,1280]{2,1,0:T(8,128)(2,1)}, u32[]{:S(2)}) copy-start(bf16[2,128,1280]{2,1,0:T(8,128)(2,1)} %get-tuple-element.164) | copy-start | bytes 1966084 | tf_op jit(solution)/shard_map/while
  586.3 0.8 copy-start.8
  647.5 11.8 %copy-start.7 = (bf16[2,128,1280]{2,1,0:T(8,128)(2,1)S(1)}, bf16[2,128,1280]{2,1,0:T(8,128)(2,1)}, u32[]{:S(2)}) copy-start(bf16[2,128,1280]{2,1,0:T(8,128)(2,1)} %get-tuple-element.164) | copy-start | bytes 1966084 | tf_op jit(solution)/shard_map/while
  659.4 0.8 copy-start.8
  660.2 4.1 copy-start.1
Sparse Core Ops, SparseCore 0:
  9.0 98.3 all-gather.2
  199.1 282.4 all-reduce.3
  483.2 39.0 all-gather.4
